TPU v7x, 512 devices: a whole 4x8x8 slice. The times are simulated.
512 devices in a mesh: gx: 32 (over x, z), gy: 16 (over y, core).
Axes of the slice: x: 4, y: 8, z: 8, core: 2. Of those that a mesh axis runs over, the one named last changes fastest.
Arguments:
- start_disp: float32 [6, 3, 128, 128, 128], P(None, None, 'gx', 'gy'), may hold values from -6 to 6
- bone_mask: int32 [128, 128, 128], P('gx', 'gy'), may hold values from 0 to 1, as said below
- density: float32 [128, 128, 128], P('gx', 'gy'), may hold values from 0.3 to 1
- load_nodes: int32 [32, 16, 6, 32], P('gx', 'gy'), may hold values from 0 to 31
- load_forces: float32 [32, 16, 6, 3, 32], P('gx', 'gy'), may hold values from -12 to 12
Outputs:
- displacement: float32 [6, 3, 128, 128, 128], P(None, None, 'gx', 'gy')
- new_density: float32 [128, 128, 128], P('gx', 'gy')
Inputs may be any that keep to these rules, and one draw needn't show every extreme that they name: `bone_mask`: 1 marks a bone voxel.
All inputs are finite; a program needn't handle non-finite values.
Results may differ from a plain program's by a relative error of at most 0.0001.
Values sent between devices are 32-bit elements; how exact they have to be, the bound alone decides.
No kernel may reach another device: no remote copies, remote signals or barrier semaphores. Data moves between devices by JAX's collectives and lax.ppermute only.
A program may use at most 64 MiB of HBM per device.

v0:
```python
import jax
import jax.numpy as jnp
import numpy as np
from jax import lax
from jax.sharding import PartitionSpec as P

spring = 0.1
poisson = 0.3
blur_sigma = 2.0
density_cap = 1.0
mean_eps = 1e-06
highest = lax.Precision.HIGHEST


def from_behind(block, axis, distance):
    devices = range(lax.axis_size(axis))
    route = [(i - distance, i) for i in devices if i - distance in devices]
    return lax.ppermute(block, axis, route)


def with_halo(cells, sides, width):
    for axis, dim in sides:
        count = lax.axis_size(axis)
        ends = count - 1
        head = lax.slice_in_dim(cells, 0, width, axis=dim)
        tail = lax.slice_in_dim(cells, cells.shape[dim] - width, cells.shape[dim], axis=dim)
        cells = jnp.concatenate(
            [
                lax.ppermute(tail, axis, [(i, (i + 1) % count) for i in range(ends)]),
                cells,
                lax.ppermute(head, axis, [((i + 1) % count, i) for i in range(ends)]),
            ],
            axis=dim,
        )
    return cells


def hex_stiffness():
    lame_first = poisson / ((1.0 + poisson) * (1.0 - 2.0 * poisson))
    shear_mod = 1.0 / (2.0 * (1.0 + poisson))
    elastic = np.zeros((6, 6))
    elastic[:3, :3] = lame_first
    for axis_id in range(3):
        elastic[axis_id, axis_id] = lame_first + 2.0 * shear_mod
        elastic[axis_id + 3, axis_id + 3] = shear_mod
    points = [0.5 - 0.5 / np.sqrt(3.0), 0.5 + 0.5 / np.sqrt(3.0)]
    stiffness = np.zeros((24, 24))
    for point_x in points:
        for point_y in points:
            for point_z in points:
                coords = (point_x, point_y, point_z)
                strain = np.zeros((6, 24))
                for corner in range(8):
                    offsets = (corner // 4, corner // 2 % 2, corner % 2)
                    shapes = [
                        coords[axis_id] if offsets[axis_id] == 1 else 1.0 - coords[axis_id]
                        for axis_id in range(3)
                    ]
                    slopes = [1.0 if offsets[axis_id] == 1 else -1.0 for axis_id in range(3)]
                    grad_x = slopes[0] * shapes[1] * shapes[2]
                    grad_y = shapes[0] * slopes[1] * shapes[2]
                    grad_z = shapes[0] * shapes[1] * slopes[2]
                    column = 3 * corner
                    strain[0, column] = grad_x
                    strain[1, column + 1] = grad_y
                    strain[2, column + 2] = grad_z
                    strain[3, column] = grad_y
                    strain[3, column + 1] = grad_x
                    strain[4, column + 1] = grad_z
                    strain[4, column + 2] = grad_y
                    strain[5, column] = grad_z
                    strain[5, column + 2] = grad_x
                stiffness += 0.125 * strain.T @ elastic @ strain
    return stiffness


def blur_weights():
    offsets = np.arange(9) - 4.0
    unscaled = np.exp(-offsets * offsets / (2.0 * blur_sigma * blur_sigma))
    return [float(entry) for entry in unscaled / unscaled.sum()]


def blur_valid(values, axis_id, extent):
    weights = blur_weights()
    summed = weights[0] * lax.slice_in_dim(values, 0, extent, axis=axis_id)
    for tap_index in range(1, 9):
        summed = summed + weights[tap_index] * lax.slice_in_dim(
            values, tap_index, tap_index + extent, axis=axis_id
        )
    return summed


def element_disp(node_field):
    size_x = node_field.shape[1] - 1
    size_y = node_field.shape[2] - 1
    size_z = node_field.shape[3] - 1
    corners = []
    for corner in range(8):
        off_x, off_y, off_z = (corner // 4, corner // 2 % 2, corner % 2)
        corners.append(
            node_field[:, off_x : off_x + size_x, off_y : off_y + size_y, off_z : off_z + size_z]
        )
    return jnp.stack(corners).reshape(24, size_x, size_y, size_z)


def element_forces(node_field, modulus, stiffness):
    local_disp = element_disp(node_field)
    local_force = jnp.einsum("ij,jabc->iabc", stiffness, local_disp, precision=highest) * modulus
    local_force = local_force.reshape((8, 3) + modulus.shape)
    summed = jnp.zeros_like(node_field)
    for corner in range(8):
        off_x, off_y, off_z = (corner // 4, corner // 2 % 2, corner % 2)
        summed = summed + jnp.pad(
            local_force[corner],
            ((0, 0), (off_x, 1 - off_x), (off_y, 1 - off_y), (off_z, 1 - off_z)),
        )
    return summed


def element_energy(node_field, stiffness):
    local_disp = element_disp(node_field)
    local_force = jnp.einsum("ij,jabc->iabc", stiffness, local_disp, precision=highest)
    return jnp.sum(local_disp * local_force, axis=0)


def local_gram(left_field, right_field):
    return jnp.einsum("iabcd,jabcd->ij", left_field, right_field, precision=highest)


def global_gram(left_field, right_field):
    return lax.psum(local_gram(left_field, right_field), ("gx", "gy"))


def mix_cases(field, coeffs):
    return jnp.einsum("kabcd,kj->jabcd", field, coeffs, precision=highest)


def solve_spd(matrix, rhs_matrix):
    factor = jnp.linalg.cholesky(matrix)
    matrix_order = matrix.shape[0]
    forward = []
    for row_index in range(matrix_order):
        partial_sum = rhs_matrix[row_index]
        for col_index in range(row_index):
            partial_sum = partial_sum - factor[row_index, col_index] * forward[col_index]
        forward.append(partial_sum / factor[row_index, row_index])
    backward = [None] * matrix_order
    for row_index in reversed(range(matrix_order)):
        partial_sum = forward[row_index]
        for col_index in range(row_index + 1, matrix_order):
            partial_sum = partial_sum - factor[col_index, row_index] * backward[col_index]
        backward[row_index] = partial_sum / factor[row_index, row_index]
    return jnp.stack(backward)


def pad_upper_z(field):
    return jnp.pad(field, ((0, 0), (0, 0), (0, 0), (0, 0), (0, 1)))


def gather_upper(field):
    from_x = from_behind(field[:, :, :1], "gx", -1)
    widened = jnp.concatenate([field, from_x], axis=2)
    from_y = from_behind(widened[:, :, :, :1], "gy", -1)
    return jnp.concatenate([widened, from_y], axis=3)


def return_lower(forces):
    size_x = forces.shape[2] - 1
    size_y = forces.shape[3] - 1
    to_y = from_behind(forces[:, :, :, size_y:], "gy", 1)
    kept = forces[:, :, :, :size_y]
    kept = jnp.concatenate([kept[:, :, :, :1] + to_y, kept[:, :, :, 1:]], axis=3)
    to_x = from_behind(kept[:, :, size_x:], "gx", 1)
    kept = kept[:, :, :size_x]
    return jnp.concatenate([kept[:, :, :1] + to_x, kept[:, :, 1:]], axis=2)


def on_device(start_disp, bone_mask, density, load_nodes, load_forces):
    stiffness = jnp.asarray(hex_stiffness(), jnp.float32)
    modulus = bone_mask.astype(jnp.float32) * density * density
    case_count = start_disp.shape[0]
    size_x = start_disp.shape[2]
    size_y = start_disp.shape[3]
    size_z = start_disp.shape[4]

    def apply_operator(field):
        node_field = pad_upper_z(gather_upper(field))
        forces = lax.map(
            lambda case_field: element_forces(case_field, modulus, stiffness), node_field
        )
        return return_lower(forces[..., :-1]) + spring * field

    slot_ids = jnp.arange(size_x * size_y, dtype=jnp.int32)
    matches = (load_nodes[0, 0][:, :, None] == slot_ids).astype(jnp.float32)
    top_plane = jnp.einsum("cls,ckl->cks", matches, load_forces[0, 0], precision=highest).reshape(
        case_count, 3, size_x, size_y
    )
    applied = apply_operator(start_disp)
    residual = jnp.concatenate(
        [-applied[..., :-1], (top_plane - applied[..., -1])[..., None]], axis=4
    )
    solution = start_disp
    norm_now = global_gram(residual, residual)
    applied = apply_operator(residual)
    step_alpha = solve_spd(global_gram(residual, applied), norm_now)
    solution = solution + mix_cases(residual, step_alpha)
    node_field = pad_upper_z(gather_upper(solution))
    energy = jnp.sum(
        lax.map(lambda case_field: element_energy(case_field, stiffness), node_field), axis=0
    )
    stimulus = modulus * energy
    smooth = blur_valid(with_halo(stimulus, (("gx", 0),), 4), 0, size_x)
    smooth = blur_valid(with_halo(smooth, (("gy", 1),), 4), 1, size_y)
    smooth = blur_valid(jnp.pad(smooth, ((0, 0), (0, 0), (4, 4))), 2, size_z)
    summed = lax.psum(jnp.sum(smooth), ("gx", "gy"))
    mean_stim = summed / (size_x * size_y * size_z * lax.axis_size("gx") * lax.axis_size("gy"))
    new_density = jnp.minimum(density * (0.5 + 0.5 * smooth / (mean_stim + mean_eps)), density_cap)
    return (solution, new_density)


def solution(mesh):
    return jax.shard_map(
        on_device,
        mesh=mesh,
        in_specs=(
            P(None, None, "gx", "gy", None),
            P("gx", "gy", None),
            P("gx", "gy", None),
            P("gx", "gy", None, None),
            P("gx", "gy", None, None, None),
        ),
        out_specs=(P(None, None, "gx", "gy", None), P("gx", "gy", None)),
        check_vma=False,
    )
```

profile of v0, /device:TPU:1, one launch (start us, length us, event | category | flops | bytes accessed | tf_op | source)
XLA Modules:
  0.0 417.8 jit_solution(12601050354318549686)
XLA Ops:
  3.8 4.3 %collective-permute-done = f32[6,3,1,8,128]{4,3,2,1,0:T(8,128)S(1)} collective-permute-done((f32[6,3,1,8,128]{4,3,2,1,0:T(8,128)S(1)}, f32[6,3,1,8,128]{4,3,2,1,0:T(8,128)S(1)}, u32[]{:S(2)}, u32[]{:S(2)}) %collective-permute-start) | collective-permute-done | bytes 73760 | tf_op jit(solution)/shard_map/ppermute | solution.py:18
  8.1 8.5 %collective-permute-start.1 = (f32[6,3,5,1,128]{4,3,2,1,0:T(1,128)S(1)}, f32[6,3,5,1,128]{4,3,2,1,0:T(1,128)S(1)}, u32[]{:S(2)}, u32[]{:S(2)}) collective-permute-start(f32[6,3,5,1,128]{4,3,2,1,0:T(1,128)S(1)} %slice.696), channel_id=1, source_target_pairs={{1,0},{2,1},{3,2},{4,3},{5,4},{6,5},{7,6},{8,7},{9,8},{10,9},{11,1... | collective-permute-start | bytes 138248 | tf_op jit(solution)/shard_map/ppermute | solution.py:18
  18.0 46.3 %while.37 = (s32[]{:T(128)}, f32[6,3,5,9,129]{4,0,3,2,1:T(8,128)S(1)}, f32[6,3,5,9,129]{4,3,2,1,0:T(8,128)S(1)}, f32[4,8,128]{2,1,0:T(8,128)S(1)}, s32[]{:T(128)}, /*index=5*/f32[24,24,1,1]{1,0,3,2:T(8,128)S(1)}, s32[]{:T(128)}) while((s32[]{:T(128)}, f32[6,3,5,9,129]{4,0,3,2,1:T(8,128)S(1)}, ...), condition=%wide.region_1.2_spmd.clone, body=%wide.region_0.1_spmd.sunk.clone.sunk | while | flops 28531760 | bytes 3258905 | solution.py:188
  19.8 5.9 %dynamic_update_slice.27 = f32[6,3,5,9,129]{4,0,3,2,1:T(8,128)S(1)} dynamic-update-slice(f32[6,3,5,9,129]{4,0,3,2,1:T(8,128)S(1)} %get-tuple-element.402, f32[1,3,5,9,129]{4,0,3,2,1:T(1,128)S(1)} %copy.116, s32[]{:T(128)} %get-tuple-element.401, s32[]{:T(128)} %constant.103.clone.1..sunk, s32[]{:T(128)} %constant.103.clone.1..sunk, s32[]{:T(128)} %constant.103.clone.1..sunk, s32[]{:T(128)} %constant.103.clone.1..sunk) | dynamic-update-slice | bytes 139324 | tf_op jit(solution)/shard_map/while/body/jit(dynamic_update_index_in_dim)/dynamic_update_slice | solution.py:188
  27.5 5.9 %dynamic_update_slice.27 = f32[6,3,5,9,129]{4,0,3,2,1:T(8,128)S(1)} dynamic-update-slice(f32[6,3,5,9,129]{4,0,3,2,1:T(8,128)S(1)} %get-tuple-element.402, f32[1,3,5,9,129]{4,0,3,2,1:T(1,128)S(1)} %copy.116, s32[]{:T(128)} %get-tuple-element.401, s32[]{:T(128)} %constant.103.clone.1..sunk, s32[]{:T(128)} %constant.103.clone.1..sunk, s32[]{:T(128)} %constant.103.clone.1..sunk, s32[]{:T(128)} %constant.103.clone.1..sunk) | dynamic-update-slice | bytes 139324 | tf_op jit(solution)/shard_map/while/body/jit(dynamic_update_index_in_dim)/dynamic_update_slice | solution.py:188
  35.2 5.9 %dynamic_update_slice.27 = f32[6,3,5,9,129]{4,0,3,2,1:T(8,128)S(1)} dynamic-update-slice(f32[6,3,5,9,129]{4,0,3,2,1:T(8,128)S(1)} %get-tuple-element.402, f32[1,3,5,9,129]{4,0,3,2,1:T(1,128)S(1)} %copy.116, s32[]{:T(128)} %get-tuple-element.401, s32[]{:T(128)} %constant.103.clone.1..sunk, s32[]{:T(128)} %constant.103.clone.1..sunk, s32[]{:T(128)} %constant.103.clone.1..sunk, s32[]{:T(128)} %constant.103.clone.1..sunk) | dynamic-update-slice | bytes 139324 | tf_op jit(solution)/shard_map/while/body/jit(dynamic_update_index_in_dim)/dynamic_update_slice | solution.py:188
  42.9 5.9 %dynamic_update_slice.27 = f32[6,3,5,9,129]{4,0,3,2,1:T(8,128)S(1)} dynamic-update-slice(f32[6,3,5,9,129]{4,0,3,2,1:T(8,128)S(1)} %get-tuple-element.402, f32[1,3,5,9,129]{4,0,3,2,1:T(1,128)S(1)} %copy.116, s32[]{:T(128)} %get-tuple-element.401, s32[]{:T(128)} %constant.103.clone.1..sunk, s32[]{:T(128)} %constant.103.clone.1..sunk, s32[]{:T(128)} %constant.103.clone.1..sunk, s32[]{:T(128)} %constant.103.clone.1..sunk) | dynamic-update-slice | bytes 139324 | tf_op jit(solution)/shard_map/while/body/jit(dynamic_update_index_in_dim)/dynamic_update_slice | solution.py:188
  50.6 5.9 %dynamic_update_slice.27 = f32[6,3,5,9,129]{4,0,3,2,1:T(8,128)S(1)} dynamic-update-slice(f32[6,3,5,9,129]{4,0,3,2,1:T(8,128)S(1)} %get-tuple-element.402, f32[1,3,5,9,129]{4,0,3,2,1:T(1,128)S(1)} %copy.116, s32[]{:T(128)} %get-tuple-element.401, s32[]{:T(128)} %constant.103.clone.1..sunk, s32[]{:T(128)} %constant.103.clone.1..sunk, s32[]{:T(128)} %constant.103.clone.1..sunk, s32[]{:T(128)} %constant.103.clone.1..sunk) | dynamic-update-slice | bytes 139324 | tf_op jit(solution)/shard_map/while/body/jit(dynamic_update_index_in_dim)/dynamic_update_slice | solution.py:188
  58.3 5.9 %dynamic_update_slice.27 = f32[6,3,5,9,129]{4,0,3,2,1:T(8,128)S(1)} dynamic-update-slice(f32[6,3,5,9,129]{4,0,3,2,1:T(8,128)S(1)} %get-tuple-element.402, f32[1,3,5,9,129]{4,0,3,2,1:T(1,128)S(1)} %copy.116, s32[]{:T(128)} %get-tuple-element.401, s32[]{:T(128)} %constant.103.clone.1..sunk, s32[]{:T(128)} %constant.103.clone.1..sunk, s32[]{:T(128)} %constant.103.clone.1..sunk, s32[]{:T(128)} %constant.103.clone.1..sunk) | dynamic-update-slice | bytes 139324 | tf_op jit(solution)/shard_map/while/body/jit(dynamic_update_index_in_dim)/dynamic_update_slice | solution.py:188
  72.9 4.8 %collective-permute-done.4 = f32[6,3,1,8,128]{4,0,3,2,1:T(8,128)S(1)} collective-permute-done((f32[6,3,1,8,128]{4,0,3,2,1:T(8,128)S(1)}, f32[6,3,1,8,128]{4,0,3,2,1:T(8,128)S(1)}, u32[]{:S(2)}, u32[]{:S(2)}) %collective-permute-start.4) | collective-permute-done | bytes 73760 | tf_op jit(solution)/shard_map/ppermute | solution.py:18
  77.8 3.6 collective-permute-start.5
  81.4 3.6 collective-permute-done.5
  85.3 47.1 %while.38 = (s32[]{:T(128)}, f32[6,3,5,9,129]{4,0,3,2,1:T(8,128)S(1)}, f32[6,3,5,9,129]{4,0,3,2,1:T(8,128)S(1)}, f32[4,8,128]{2,1,0:T(8,128)S(1)}, s32[]{:T(128)}, /*index=5*/f32[24,24,1,1]{1,0,3,2:T(8,128)S(1)}, s32[]{:T(128)}) while((s32[]{:T(128)}, f32[6,3,5,9,129]{4,0,3,2,1:T(8,128)S(1)}, ...), condition=%wide.region_4.5_spmd.clone, body=%wide.region_3.4_spmd.sunk.clone.sunk | while | flops 28531760 | bytes 3398225 | solution.py:188
  87.2 5.9 %dynamic_update_slice.28 = f32[6,3,5,9,129]{4,0,3,2,1:T(8,128)S(1)} dynamic-update-slice(f32[6,3,5,9,129]{4,0,3,2,1:T(8,128)S(1)} %get-tuple-element.423, f32[1,3,5,9,129]{4,0,3,2,1:T(1,128)S(1)} %copy.119, s32[]{:T(128)} %get-tuple-element.422, s32[]{:T(128)} %constant.103.clone.1..sunk.1, s32[]{:T(128)} %constant.103.clone.1..sunk.1, s32[]{:T(128)} %constant.103.clone.1..sunk.1, ...) | dynamic-update-slice | bytes 139324 | tf_op jit(solution)/shard_map/while/body/jit(dynamic_update_index_in_dim)/dynamic_update_slice | solution.py:188
  95.1 5.9 %dynamic_update_slice.28 = f32[6,3,5,9,129]{4,0,3,2,1:T(8,128)S(1)} dynamic-update-slice(f32[6,3,5,9,129]{4,0,3,2,1:T(8,128)S(1)} %get-tuple-element.423, f32[1,3,5,9,129]{4,0,3,2,1:T(1,128)S(1)} %copy.119, s32[]{:T(128)} %get-tuple-element.422, s32[]{:T(128)} %constant.103.clone.1..sunk.1, s32[]{:T(128)} %constant.103.clone.1..sunk.1, s32[]{:T(128)} %constant.103.clone.1..sunk.1, ...) | dynamic-update-slice | bytes 139324 | tf_op jit(solution)/shard_map/while/body/jit(dynamic_update_index_in_dim)/dynamic_update_slice | solution.py:188
  102.9 5.9 %dynamic_update_slice.28 = f32[6,3,5,9,129]{4,0,3,2,1:T(8,128)S(1)} dynamic-update-slice(f32[6,3,5,9,129]{4,0,3,2,1:T(8,128)S(1)} %get-tuple-element.423, f32[1,3,5,9,129]{4,0,3,2,1:T(1,128)S(1)} %copy.119, s32[]{:T(128)} %get-tuple-element.422, s32[]{:T(128)} %constant.103.clone.1..sunk.1, s32[]{:T(128)} %constant.103.clone.1..sunk.1, s32[]{:T(128)} %constant.103.clone.1..sunk.1, ...) | dynamic-update-slice | bytes 139324 | tf_op jit(solution)/shard_map/while/body/jit(dynamic_update_index_in_dim)/dynamic_update_slice | solution.py:188
  110.7 5.9 %dynamic_update_slice.28 = f32[6,3,5,9,129]{4,0,3,2,1:T(8,128)S(1)} dynamic-update-slice(f32[6,3,5,9,129]{4,0,3,2,1:T(8,128)S(1)} %get-tuple-element.423, f32[1,3,5,9,129]{4,0,3,2,1:T(1,128)S(1)} %copy.119, s32[]{:T(128)} %get-tuple-element.422, s32[]{:T(128)} %constant.103.clone.1..sunk.1, s32[]{:T(128)} %constant.103.clone.1..sunk.1, s32[]{:T(128)} %constant.103.clone.1..sunk.1, ...) | dynamic-update-slice | bytes 139324 | tf_op jit(solution)/shard_map/while/body/jit(dynamic_update_index_in_dim)/dynamic_update_slice | solution.py:188
  118.6 5.9 %dynamic_update_slice.28 = f32[6,3,5,9,129]{4,0,3,2,1:T(8,128)S(1)} dynamic-update-slice(f32[6,3,5,9,129]{4,0,3,2,1:T(8,128)S(1)} %get-tuple-element.423, f32[1,3,5,9,129]{4,0,3,2,1:T(1,128)S(1)} %copy.119, s32[]{:T(128)} %get-tuple-element.422, s32[]{:T(128)} %constant.103.clone.1..sunk.1, s32[]{:T(128)} %constant.103.clone.1..sunk.1, s32[]{:T(128)} %constant.103.clone.1..sunk.1, ...) | dynamic-update-slice | bytes 139324 | tf_op jit(solution)/shard_map/while/body/jit(dynamic_update_index_in_dim)/dynamic_update_slice | solution.py:188
  126.4 5.9 %dynamic_update_slice.28 = f32[6,3,5,9,129]{4,0,3,2,1:T(8,128)S(1)} dynamic-update-slice(f32[6,3,5,9,129]{4,0,3,2,1:T(8,128)S(1)} %get-tuple-element.423, f32[1,3,5,9,129]{4,0,3,2,1:T(1,128)S(1)} %copy.119, s32[]{:T(128)} %get-tuple-element.422, s32[]{:T(128)} %constant.103.clone.1..sunk.1, s32[]{:T(128)} %constant.103.clone.1..sunk.1, s32[]{:T(128)} %constant.103.clone.1..sunk.1, ...) | dynamic-update-slice | bytes 139324 | tf_op jit(solution)/shard_map/while/body/jit(dynamic_update_index_in_dim)/dynamic_update_slice | solution.py:188
  132.4 1.9 collective-permute-start.6
  135.6 4.7 %collective-permute-start.7 = (f32[6,3,1,8,128]{4,0,3,2,1:T(8,128)S(1)}, f32[6,3,1,8,128]{4,0,3,2,1:T(8,128)S(1)}, u32[]{:S(2)}, u32[]{:S(2)}) collective-permute-start(f32[6,3,1,8,128]{4,0,3,2,1:T(8,128)S(1)} %pad_maximum_fusion.1), channel_id=1, source_target_pairs={{0,16},{16,32},{32,48},{48,64},{64,80},{80,96},{96,112},{112,128},... | collective-permute-start | bytes 221192 | tf_op jit(solution)/shard_map/ppermute | solution.py:18
  143.5 108.2 %all-reduce.20 = (f32[6,6]{1,0:T(8,128)S(1)}, f32[6,6]{0,1:T(8,128)S(1)}) all-reduce(f32[6,6]{1,0:T(8,128)S(1)} %convolution_bitcast_fusion.2, f32[6,6]{0,1:T(8,128)S(1)} %convolution_bitcast_fusion.1), channel_id=1, replica_groups=mesh['gx'=32,'gy'=16] {'gx','gy'}, use_global_device_ids=true, to_apply=%region_2.3 | all-reduce | flops 72 | bytes 576 | tf_op jit(solution)/shard_map/psum | solution.py:131
  256.3 9.5 %subtract_divide_fusion.6 = (f32[1,6]{1,0:T(1,128)S(1)}, f32[1,6]{1,0:T(1,128)S(1)}, f32[1,6]{1,0:T(1,128)S(1)}, f32[1,6]{1,0:T(1,128)S(1)}, f32[1,6]{1,0:T(1,128)S(1)}) fusion(f32[6,6]{1,0:T(8,128)S(1)} %get-tuple-element.239, f32[]{:T(128)} %bitcast.19, f32[]{:T(128)} %bitcast.18, f32[]{:T(128)} %bitcast.17, f32[]{:T(128)} %bitcast.16, f32[]{:T(128)} %bitcast.15, ...), kind=kLoop, calls=%fused_computation.219 | loop fusion | flops 150 | bytes 300 | tf_op jit(solution)/shard_map/div | solution.py:146
  265.8 12.6 %subtract_divide_fusion = (f32[1,6]{1,0:T(1,128)S(1)}, f32[1,6]{1,0:T(1,128)S(1)}, f32[1,6]{1,0:T(1,128)S(1)}, f32[1,6]{1,0:T(1,128)S(1)}, f32[1,6]{1,0:T(1,128)S(1)}, /*index=5*/f32[1,6]{1,0:T(1,128)S(1)}) fusion(f32[1,6]{1,0:T(1,128)S(1)} %get-tuple-element.253, f32[]{:T(128)} %bitcast.21, f32[]{:T(128)} %bitcast.16, f32[]{:T(128)} %bitcast.12, ...), kind=kLoop, calls=%fused_computation.213 | loop fusion | flops 276 | bytes 372 | tf_op jit(solution)/shard_map/div | solution.py:152
  280.6 4.1 collective-permute-done.8
  284.6 3.7 collective-permute-start.9
  288.4 3.8 collective-permute-done.9
  292.3 8.5 %while.39 = (s32[]{:T(128)}, f32[6,4,8,128]{3,2,1,0:T(8,128)S(1)}, f32[6,3,5,9,129]{4,0,3,2,1:T(8,128)S(1)}, s32[]{:T(128)}, f32[24,24,1,1]{1,0,3,2:T(8,128)S(1)}) while((s32[]{:T(128)}, f32[6,4,8,128]{3,2,1,0:T(8,128)S(1)}, f32[6,3,5,9,129]{4,0,3,2,1:T(8,128)S(1)}, s32[]{:T(128)}, f32[24,24,1,1]{1,0,3,2:T(8,128)S(1)}) %tuple.141), condition=%wide.region_10.11_spmd.clone, body=%wide.region_8.10_spmd.sunk.clone.sunk | while | flops 28504064 | bytes 1509813 | solution.py:209
  303.5 3.4 collective-permute-done.11
  306.9 3.0 collective-permute-start.12
  312.6 2.3 collective-permute-done.13
  315.7 100.9 %psum.23 = f32[]{:T(128)} all-reduce(f32[]{:T(128)} %get-tuple-element.241), channel_id=1, replica_groups=mesh['gx'=32,'gy'=16] {'gx','gy'}, use_global_device_ids=true, to_apply=%region_13.14 | all-reduce | flops 1 | bytes 8 | tf_op jit(solution)/shard_map/psum | solution.py:215
  (311 shorter events, 58.9 us)
Async XLA Ops:
  1.5 6.6 %collective-permute-start = (f32[6,3,1,8,128]{4,3,2,1,0:T(8,128)S(1)}, f32[6,3,1,8,128]{4,3,2,1,0:T(8,128)S(1)}, u32[]{:S(2)}, u32[]{:S(2)}) collective-permute-start(f32[6,3,1,8,128]{4,3,2,1,0:T(8,128)S(1)} %slice.505), channel_id=1, source_target_pairs={{16,0},{32,16},{48,32},{64,48},{80,64},{96,80},{112,96},{128,112},... | collective-permute-start | bytes 221192 | tf_op jit(solution)/shard_map/ppermute | solution.py:18
  8.1 9.3 %collective-permute-start.1 = (f32[6,3,5,1,128]{4,3,2,1,0:T(1,128)S(1)}, f32[6,3,5,1,128]{4,3,2,1,0:T(1,128)S(1)}, u32[]{:S(2)}, u32[]{:S(2)}) collective-permute-start(f32[6,3,5,1,128]{4,3,2,1,0:T(1,128)S(1)} %slice.696), channel_id=1, source_target_pairs={{1,0},{2,1},{3,2},{4,3},{5,4},{6,5},{7,6},{8,7},{9,8},{10,9},{11,1... | collective-permute-start | bytes 138248 | tf_op jit(solution)/shard_map/ppermute | solution.py:18
  17.3 0.7 copy-start.1
  18.0 48.2 %copy-start.3 = (s32[1,1,6,32]{3,1,2,0:T(1,128)S(1)}, s32[1,1,6,32]{3,1,2,0:T(1,128)}, u32[]{:S(2)}) copy-start(s32[1,1,6,32]{3,1,2,0:T(1,128)} %param.15) | copy-start | bytes 2308
  64.3 4.6 %copy-start.4 = (f32[1,1,6,3,32]{4,1,3,2,0:T(1,128)S(1)}, f32[1,1,6,3,32]{4,1,3,2,0:T(1,128)}, u32[]{:S(2)}) copy-start(f32[1,1,6,3,32]{4,1,3,2,0:T(1,128)} %param.16) | copy-start | bytes 6916
  64.3 3.2 collective-permute-start.2
  66.3 4.7 %copy-start = (f32[6,3,4,8,128]{4,3,2,1,0:T(8,128)S(1)}, f32[6,3,4,8,128]{4,3,2,1,0:T(8,128)}, u32[]{:S(2)}) copy-start(f32[6,3,4,8,128]{4,3,2,1,0:T(8,128)} %param.12) | copy-start | bytes 884740
  67.6 3.4 collective-permute-start.3
  71.6 6.1 %collective-permute-start.4 = (f32[6,3,1,8,128]{4,0,3,2,1:T(8,128)S(1)}, f32[6,3,1,8,128]{4,0,3,2,1:T(8,128)S(1)}, u32[]{:S(2)}, u32[]{:S(2)}) collective-permute-start(f32[6,3,1,8,128]{4,0,3,2,1:T(8,128)S(1)} %fusion.43), channel_id=1, source_target_pairs={{16,0},{32,16},{48,32},{64,48},{80,64},{96,80},{112,96},{128,112},... | collective-permute-start | bytes 221192 | tf_op jit(solution)/shard_map/ppermute | solution.py:18
  77.8 7.3 %collective-permute-start.5 = (f32[6,3,5,1,128]{4,0,3,2,1:T(8,128)S(1)}, f32[6,3,5,1,128]{4,0,3,2,1:T(8,128)S(1)}, u32[]{:S(2)}, u32[]{:S(2)}) collective-permute-start(f32[6,3,5,1,128]{4,0,3,2,1:T(8,128)S(1)} %pad_maximum_fusion.4), channel_id=1, source_target_pairs={{1,0},{2,1},{3,2},{4,3},{5,4},{6,5},{7,6},{8,7},{9,8},{10,9},{11,1... | collective-permute-start | bytes 138248 | tf_op jit(solution)/shard_map/ppermute | solution.py:18
  132.4 3.2 collective-permute-start.6
  135.6 6.8 %collective-permute-start.7 = (f32[6,3,1,8,128]{4,0,3,2,1:T(8,128)S(1)}, f32[6,3,1,8,128]{4,0,3,2,1:T(8,128)S(1)}, u32[]{:S(2)}, u32[]{:S(2)}) collective-permute-start(f32[6,3,1,8,128]{4,0,3,2,1:T(8,128)S(1)} %pad_maximum_fusion.1), channel_id=1, source_target_pairs={{0,16},{16,32},{32,48},{48,64},{64,80},{80,96},{96,112},{112,128},... | collective-permute-start | bytes 221192 | tf_op jit(solution)/shard_map/ppermute | solution.py:18
  279.3 5.4 %collective-permute-start.8 = (f32[6,3,1,8,128]{4,0,3,2,1:T(8,128)S(1)}, f32[6,3,1,8,128]{4,0,3,2,1:T(8,128)S(1)}, u32[]{:S(2)}, u32[]{:S(2)}) collective-permute-start(f32[6,3,1,8,128]{4,0,3,2,1:T(8,128)S(1)} %slice.701), channel_id=1, source_target_pairs={{16,0},{32,16},{48,32},{64,48},{80,64},{96,80},{112,96},{128,112},... | collective-permute-start | bytes 221192 | tf_op jit(solution)/shard_map/ppermute | solution.py:18
  284.6 7.5 %collective-permute-start.9 = (f32[6,3,5,1,128]{4,0,3,2,1:T(8,128)S(1)}, f32[6,3,5,1,128]{4,0,3,2,1:T(8,128)S(1)}, u32[]{:S(2)}, u32[]{:S(2)}) collective-permute-start(f32[6,3,5,1,128]{4,0,3,2,1:T(8,128)S(1)} %pad_maximum_fusion.3), channel_id=1, source_target_pairs={{1,0},{2,1},{3,2},{4,3},{5,4},{6,5},{7,6},{8,7},{9,8},{10,9},{11,1... | collective-permute-start | bytes 138248 | tf_op jit(solution)/shard_map/ppermute | solution.py:18
  292.3 124.9 %copy-start.2 = (f32[4,8,128]{2,1,0:T(8,128)S(1)}, f32[4,8,128]{2,1,0:T(8,128)}, u32[]{:S(2)}) copy-start(f32[4,8,128]{2,1,0:T(8,128)} %param.14) | copy-start | bytes 49156
  300.8 2.6 collective-permute-start.10
  302.1 4.7 %collective-permute-start.11 = (f32[4,8,128]{2,1,0:T(8,128)S(1)}, f32[4,8,128]{2,1,0:T(8,128)S(1)}, u32[]{:S(2)}, u32[]{:S(2)}) collective-permute-start(f32[4,8,128]{2,1,0:T(8,128)S(1)} %mul.463), channel_id=1, source_target_pairs={{16,0},{32,16},{48,32},{64,48},{80,64},{96,80},{112,96},{128,112},... | collective-permute-start | bytes 49160 | tf_op jit(solution)/shard_map/ppermute | solution.py:31
  306.9 5.7 %collective-permute-start.12 = (f32[4,4,128]{2,1,0:T(4,128)S(1)}, f32[4,4,128]{2,1,0:T(4,128)S(1)}, u32[]{:S(2)}, u32[]{:S(2)}) collective-permute-start(f32[4,4,128]{2,1,0:T(4,128)S(1)} %get-tuple-element.270), channel_id=1, source_target_pairs={{0,1},{1,2},{2,3},{3,4},{4,5},{5,6},{6,7},{7,8},{8,9},{9,10},{10,1... | collective-permute-start | bytes 24584 | tf_op jit(solution)/shard_map/ppermute | solution.py:29
  309.9 5.0 %collective-permute-start.13 = (f32[4,4,128]{2,1,0:T(4,128)S(1)}, f32[4,4,128]{2,1,0:T(4,128)S(1)}, u32[]{:S(2)}, u32[]{:S(2)}) collective-permute-start(f32[4,4,128]{2,1,0:T(4,128)S(1)} %get-tuple-element.271), channel_id=1, source_target_pairs={{1,0},{2,1},{3,2},{4,3},{5,4},{6,5},{7,6},{8,7},{9,8},{10,9},{11,1... | collective-permute-start | bytes 24584 | tf_op jit(solution)/shard_map/ppermute | solution.py:31
where the time goes:
time: 419 us; the launch traced here: 418 us
  blocking collectives  209 us (50%)
  local copies, waits for them, and re-layouts  88.3 us (21%)
  starting transfers between devices  37.1 us (9%)
  other arithmetic  31.3 us (7%)
  waiting for transfers between devices  31.1 us (7%)
  matrix products  16.5 us (4%)
    psum x1, blocking collectives, global_gram(): return lax.psum(local_gram(left_field, right_field), ('gx', 'gy'))  108 us
    psum x1, blocking collectives, on_device(): summed = lax.psum(jnp.sum(smooth), ('gx', 'gy'))  101 us
    dynamic_update_slice x24, local copies, waits for them, and re-layouts, apply_operator(): lax.map(lambda case_field: element_forces(case_field, modulus, stiffness)...  73.1 us
    ppermute x10, starting transfers between devices, from_behind(): return lax.ppermute(block, axis, route)  29.5 us
    ppermute x10, waiting for transfers between devices, from_behind(): return lax.ppermute(block, axis, route)  25.4 us
    div x1, other arithmetic, solve_spd(): backward[row_index] = partial_sum / factor[row_index, row_index]  12.6 us
    div x1, other arithmetic, solve_spd(): forward.append(partial_sum / factor[row_index, row_index])  9.49 us
  transfers between devices with their start and end apart: 14, of which 12 were waited for; matrix products, arithmetic and copies ran while one was open for 1% of the time, Pallas kernels for 0%

commit v1 on v0

--- a/solution.py
+++ b/solution.py
@@ -128,7 +128,7 @@
 
 
 def global_gram(left_field, right_field):
-    return lax.psum(local_gram(left_field, right_field), ("gx", "gy"))
+    return jnp.sum(lax.all_gather(local_gram(left_field, right_field), ("gx", "gy")), axis=0)
 
 
 def mix_cases(field, coeffs):

time: 419 us -> 462 us (1.10)
  blocking collectives: 209 us -> 255 us
    all_gather x0 -> x2, blocking collectives: none -> 154 us  [global_gram(): lax.all_gather(local_gram(left_field, right_field), ('gx', 'gy'))]
    psum x1 -> x0, blocking collectives: 108 us -> none  [global_gram(): return lax.psum(local_gram(left_field, right_field), ('gx', 'gy'))]
    div x1 -> x0, other arithmetic: 9.49 us -> none  [solve_spd(): forward.append(partial_sum / factor[row_index, row_index])]
    div x1 -> x2, other arithmetic: 12.6 us -> 19.4 us  [solve_spd(): backward[row_index] = partial_sum / factor[row_index, row_index]]
  transfers between devices with their start and end apart: 14 -> 14, of which waited for: 12 -> 11; matrix products, arithmetic and copies ran while one was open for 1% -> 1% of each run, Pallas kernels for 0% -> 0%
where the time goes in v1:
time: 462 us; the launch traced here: 461 us
  blocking collectives  255 us (55%)
  local copies, waits for them, and re-layouts  90.5 us (20%)
  starting transfers between devices  34.7 us (8%)
  other arithmetic  30.5 us (7%)
  waiting for transfers between devices  29.7 us (6%)
  matrix products  16.5 us (4%)
    all_gather x2, blocking collectives, global_gram(): lax.all_gather(local_gram(left_field, right_field), ('gx', 'gy'))  154 us
    psum x1, blocking collectives, on_device(): summed = lax.psum(jnp.sum(smooth), ('gx', 'gy'))  101 us
    dynamic_update_slice x24, local copies, waits for them, and re-layouts, apply_operator(): lax.map(lambda case_field: element_forces(case_field, modulus, stiffness)...  73.1 us
    ppermute x10, starting transfers between devices, from_behind(): return lax.ppermute(block, axis, route)  25.5 us
    ppermute x10, waiting for transfers between devices, from_behind(): return lax.ppermute(block, axis, route)  24.2 us
    div x2, other arithmetic, solve_spd(): backward[row_index] = partial_sum / factor[row_index, row_index]  19.4 us
  transfers between devices with their start and end apart: 14, of which 11 were waited for; matrix products, arithmetic and copies ran while one was open for 1% of the time, Pallas kernels for 0%

profile of v1, /device:TPU:1, one launch (start us, length us, event | category | flops | bytes accessed | tf_op | source)
XLA Modules:
  0.0 461.3 jit_solution(9038167937229230319)
XLA Ops:
  3.8 4.3 collective-permute-done
  8.1 8.5 %collective-permute-start.1 = (f32[6,3,5,1,128]{4,3,2,1,0:T(1,128)S(1)}, f32[6,3,5,1,128]{4,3,2,1,0:T(1,128)S(1)}, u32[]{:S(2)}, u32[]{:S(2)}) collective-permute-start(f32[6,3,5,1,128]{4,3,2,1,0:T(1,128)S(1)} %slice.696), channel_id=1, source_target_pairs={{1,0},{2,1},{3,2},{4,3},{5,4},{6,5},{7,6},{8,7},{9,8},{10,9},{11,1... | collective-permute-start | bytes 138248 | tf_op jit(solution)/shard_map/ppermute | solution.py:18
  18.0 46.3 %while.37 = (s32[]{:T(128)}, f32[6,3,5,9,129]{4,0,3,2,1:T(8,128)S(1)}, f32[6,3,5,9,129]{4,3,2,1,0:T(8,128)S(1)}, f32[4,8,128]{2,1,0:T(8,128)S(1)}, s32[]{:T(128)}, /*index=5*/f32[24,24,1,1]{1,0,3,2:T(8,128)S(1)}, s32[]{:T(128)}) while((s32[]{:T(128)}, f32[6,3,5,9,129]{4,0,3,2,1:T(8,128)S(1)}, ...), condition=%wide.region_1.2_spmd.clone, body=%wide.region_0.1_spmd.sunk.clone.sunk | while | flops 28531760 | bytes 3258905 | solution.py:188
  19.8 5.9 %dynamic_update_slice.27 = f32[6,3,5,9,129]{4,0,3,2,1:T(8,128)S(1)} dynamic-update-slice(f32[6,3,5,9,129]{4,0,3,2,1:T(8,128)S(1)} %get-tuple-element.409, f32[1,3,5,9,129]{4,0,3,2,1:T(1,128)S(1)} %copy.141, s32[]{:T(128)} %get-tuple-element.408, s32[]{:T(128)} %constant.103.clone.1..sunk, s32[]{:T(128)} %constant.103.clone.1..sunk, s32[]{:T(128)} %constant.103.clone.1..sunk, s32[]{:T(128)} %constant.103.clone.1..sunk) | dynamic-update-slice | bytes 139324 | tf_op jit(solution)/shard_map/while/body/jit(dynamic_update_index_in_dim)/dynamic_update_slice | solution.py:188
  27.5 5.9 %dynamic_update_slice.27 = f32[6,3,5,9,129]{4,0,3,2,1:T(8,128)S(1)} dynamic-update-slice(f32[6,3,5,9,129]{4,0,3,2,1:T(8,128)S(1)} %get-tuple-element.409, f32[1,3,5,9,129]{4,0,3,2,1:T(1,128)S(1)} %copy.141, s32[]{:T(128)} %get-tuple-element.408, s32[]{:T(128)} %constant.103.clone.1..sunk, s32[]{:T(128)} %constant.103.clone.1..sunk, s32[]{:T(128)} %constant.103.clone.1..sunk, s32[]{:T(128)} %constant.103.clone.1..sunk) | dynamic-update-slice | bytes 139324 | tf_op jit(solution)/shard_map/while/body/jit(dynamic_update_index_in_dim)/dynamic_update_slice | solution.py:188
  35.2 5.9 %dynamic_update_slice.27 = f32[6,3,5,9,129]{4,0,3,2,1:T(8,128)S(1)} dynamic-update-slice(f32[6,3,5,9,129]{4,0,3,2,1:T(8,128)S(1)} %get-tuple-element.409, f32[1,3,5,9,129]{4,0,3,2,1:T(1,128)S(1)} %copy.141, s32[]{:T(128)} %get-tuple-element.408, s32[]{:T(128)} %constant.103.clone.1..sunk, s32[]{:T(128)} %constant.103.clone.1..sunk, s32[]{:T(128)} %constant.103.clone.1..sunk, s32[]{:T(128)} %constant.103.clone.1..sunk) | dynamic-update-slice | bytes 139324 | tf_op jit(solution)/shard_map/while/body/jit(dynamic_update_index_in_dim)/dynamic_update_slice | solution.py:188
  42.9 5.9 %dynamic_update_slice.27 = f32[6,3,5,9,129]{4,0,3,2,1:T(8,128)S(1)} dynamic-update-slice(f32[6,3,5,9,129]{4,0,3,2,1:T(8,128)S(1)} %get-tuple-element.409, f32[1,3,5,9,129]{4,0,3,2,1:T(1,128)S(1)} %copy.141, s32[]{:T(128)} %get-tuple-element.408, s32[]{:T(128)} %constant.103.clone.1..sunk, s32[]{:T(128)} %constant.103.clone.1..sunk, s32[]{:T(128)} %constant.103.clone.1..sunk, s32[]{:T(128)} %constant.103.clone.1..sunk) | dynamic-update-slice | bytes 139324 | tf_op jit(solution)/shard_map/while/body/jit(dynamic_update_index_in_dim)/dynamic_update_slice | solution.py:188
  50.6 5.9 %dynamic_update_slice.27 = f32[6,3,5,9,129]{4,0,3,2,1:T(8,128)S(1)} dynamic-update-slice(f32[6,3,5,9,129]{4,0,3,2,1:T(8,128)S(1)} %get-tuple-element.409, f32[1,3,5,9,129]{4,0,3,2,1:T(1,128)S(1)} %copy.141, s32[]{:T(128)} %get-tuple-element.408, s32[]{:T(128)} %constant.103.clone.1..sunk, s32[]{:T(128)} %constant.103.clone.1..sunk, s32[]{:T(128)} %constant.103.clone.1..sunk, s32[]{:T(128)} %constant.103.clone.1..sunk) | dynamic-update-slice | bytes 139324 | tf_op jit(solution)/shard_map/while/body/jit(dynamic_update_index_in_dim)/dynamic_update_slice | solution.py:188
  58.3 5.9 %dynamic_update_slice.27 = f32[6,3,5,9,129]{4,0,3,2,1:T(8,128)S(1)} dynamic-update-slice(f32[6,3,5,9,129]{4,0,3,2,1:T(8,128)S(1)} %get-tuple-element.409, f32[1,3,5,9,129]{4,0,3,2,1:T(1,128)S(1)} %copy.141, s32[]{:T(128)} %get-tuple-element.408, s32[]{:T(128)} %constant.103.clone.1..sunk, s32[]{:T(128)} %constant.103.clone.1..sunk, s32[]{:T(128)} %constant.103.clone.1..sunk, s32[]{:T(128)} %constant.103.clone.1..sunk) | dynamic-update-slice | bytes 139324 | tf_op jit(solution)/shard_map/while/body/jit(dynamic_update_index_in_dim)/dynamic_update_slice | solution.py:188
  72.9 4.8 %collective-permute-done.4 = f32[6,3,1,8,128]{4,0,3,2,1:T(8,128)S(1)} collective-permute-done((f32[6,3,1,8,128]{4,0,3,2,1:T(8,128)S(1)}, f32[6,3,1,8,128]{4,0,3,2,1:T(8,128)S(1)}, u32[]{:S(2)}, u32[]{:S(2)}) %collective-permute-start.4) | collective-permute-done | bytes 73760 | tf_op jit(solution)/shard_map/ppermute | solution.py:18
  77.8 3.6 collective-permute-start.5
  81.4 3.6 collective-permute-done.5
  85.3 47.1 %while.38 = (s32[]{:T(128)}, f32[6,3,5,9,129]{4,0,3,2,1:T(8,128)S(1)}, f32[6,3,5,9,129]{4,0,3,2,1:T(8,128)S(1)}, f32[4,8,128]{2,1,0:T(8,128)S(1)}, s32[]{:T(128)}, /*index=5*/f32[24,24,1,1]{1,0,3,2:T(8,128)S(1)}, s32[]{:T(128)}) while((s32[]{:T(128)}, f32[6,3,5,9,129]{4,0,3,2,1:T(8,128)S(1)}, ...), condition=%wide.region_4.5_spmd.clone, body=%wide.region_3.4_spmd.sunk.clone.sunk | while | flops 28531760 | bytes 3398225 | solution.py:188
  87.2 5.9 %dynamic_update_slice.28 = f32[6,3,5,9,129]{4,0,3,2,1:T(8,128)S(1)} dynamic-update-slice(f32[6,3,5,9,129]{4,0,3,2,1:T(8,128)S(1)} %get-tuple-element.430, f32[1,3,5,9,129]{4,0,3,2,1:T(1,128)S(1)} %copy.144, s32[]{:T(128)} %get-tuple-element.429, s32[]{:T(128)} %constant.103.clone.1..sunk.1, s32[]{:T(128)} %constant.103.clone.1..sunk.1, s32[]{:T(128)} %constant.103.clone.1..sunk.1, ...) | dynamic-update-slice | bytes 139324 | tf_op jit(solution)/shard_map/while/body/jit(dynamic_update_index_in_dim)/dynamic_update_slice | solution.py:188
  95.1 5.9 %dynamic_update_slice.28 = f32[6,3,5,9,129]{4,0,3,2,1:T(8,128)S(1)} dynamic-update-slice(f32[6,3,5,9,129]{4,0,3,2,1:T(8,128)S(1)} %get-tuple-element.430, f32[1,3,5,9,129]{4,0,3,2,1:T(1,128)S(1)} %copy.144, s32[]{:T(128)} %get-tuple-element.429, s32[]{:T(128)} %constant.103.clone.1..sunk.1, s32[]{:T(128)} %constant.103.clone.1..sunk.1, s32[]{:T(128)} %constant.103.clone.1..sunk.1, ...) | dynamic-update-slice | bytes 139324 | tf_op jit(solution)/shard_map/while/body/jit(dynamic_update_index_in_dim)/dynamic_update_slice | solution.py:188
  102.9 5.9 %dynamic_update_slice.28 = f32[6,3,5,9,129]{4,0,3,2,1:T(8,128)S(1)} dynamic-update-slice(f32[6,3,5,9,129]{4,0,3,2,1:T(8,128)S(1)} %get-tuple-element.430, f32[1,3,5,9,129]{4,0,3,2,1:T(1,128)S(1)} %copy.144, s32[]{:T(128)} %get-tuple-element.429, s32[]{:T(128)} %constant.103.clone.1..sunk.1, s32[]{:T(128)} %constant.103.clone.1..sunk.1, s32[]{:T(128)} %constant.103.clone.1..sunk.1, ...) | dynamic-update-slice | bytes 139324 | tf_op jit(solution)/shard_map/while/body/jit(dynamic_update_index_in_dim)/dynamic_update_slice | solution.py:188
  110.7 5.9 %dynamic_update_slice.28 = f32[6,3,5,9,129]{4,0,3,2,1:T(8,128)S(1)} dynamic-update-slice(f32[6,3,5,9,129]{4,0,3,2,1:T(8,128)S(1)} %get-tuple-element.430, f32[1,3,5,9,129]{4,0,3,2,1:T(1,128)S(1)} %copy.144, s32[]{:T(128)} %get-tuple-element.429, s32[]{:T(128)} %constant.103.clone.1..sunk.1, s32[]{:T(128)} %constant.103.clone.1..sunk.1, s32[]{:T(128)} %constant.103.clone.1..sunk.1, ...) | dynamic-update-slice | bytes 139324 | tf_op jit(solution)/shard_map/while/body/jit(dynamic_update_index_in_dim)/dynamic_update_slice | solution.py:188
  118.6 5.9 %dynamic_update_slice.28 = f32[6,3,5,9,129]{4,0,3,2,1:T(8,128)S(1)} dynamic-update-slice(f32[6,3,5,9,129]{4,0,3,2,1:T(8,128)S(1)} %get-tuple-element.430, f32[1,3,5,9,129]{4,0,3,2,1:T(1,128)S(1)} %copy.144, s32[]{:T(128)} %get-tuple-element.429, s32[]{:T(128)} %constant.103.clone.1..sunk.1, s32[]{:T(128)} %constant.103.clone.1..sunk.1, s32[]{:T(128)} %constant.103.clone.1..sunk.1, ...) | dynamic-update-slice | bytes 139324 | tf_op jit(solution)/shard_map/while/body/jit(dynamic_update_index_in_dim)/dynamic_update_slice | solution.py:188
  126.4 5.9 %dynamic_update_slice.28 = f32[6,3,5,9,129]{4,0,3,2,1:T(8,128)S(1)} dynamic-update-slice(f32[6,3,5,9,129]{4,0,3,2,1:T(8,128)S(1)} %get-tuple-element.430, f32[1,3,5,9,129]{4,0,3,2,1:T(1,128)S(1)} %copy.144, s32[]{:T(128)} %get-tuple-element.429, s32[]{:T(128)} %constant.103.clone.1..sunk.1, s32[]{:T(128)} %constant.103.clone.1..sunk.1, s32[]{:T(128)} %constant.103.clone.1..sunk.1, ...) | dynamic-update-slice | bytes 139324 | tf_op jit(solution)/shard_map/while/body/jit(dynamic_update_index_in_dim)/dynamic_update_slice | solution.py:188
  136.1 81.1 %all-gather.2 = f32[512,6,6]{2,1,0:T(8,128)S(1)} all-gather(f32[1,6,6]{2,1,0:T(8,128)S(1)} %convolution_bitcast_fusion.2), channel_id=2, replica_groups=mesh['gx'=32,'gy'=16] {'gx','gy'}, dimensions={0}, use_global_device_ids=true | all-gather | bytes 73872 | tf_op jit(solution)/shard_map/all_gather | solution.py:131
  224.4 73.3 %all-gather.3 = f32[512,6,6]{2,1,0:T(8,128)S(1)} all-gather(f32[1,6,6]{2,1,0:T(8,128)S(1)} %convolution_bitcast_fusion.1), channel_id=3, replica_groups=mesh['gx'=32,'gy'=16] {'gx','gy'}, dimensions={0}, use_global_device_ids=true | all-gather | bytes 73872 | tf_op jit(solution)/shard_map/all_gather | solution.py:131
  302.6 12.6 %subtract_divide_fusion.1 = (f32[1,6]{0,1:T(8,128)S(1)}, f32[1,6]{0,1:T(8,128)S(1)}, f32[1,6]{0,1:T(8,128)S(1)}, f32[1,6]{0,1:T(8,128)S(1)}, f32[1,6]{0,1:T(8,128)S(1)}) fusion(f32[]{:T(128)} %bitcast.25, f32[]{:T(128)} %bitcast.20, f32[]{:T(128)} %bitcast.16, f32[]{:T(128)} %bitcast.11, f32[]{:T(128)} %bitcast.10, f32[1,6]{0,1:T(8,128)S(1)} %copy.99, ...), kind=kLoop, calls=%fused_computation.209 | loop fusion | flops 360 | bytes 348 | tf_op jit(solution)/shard_map/div | solution.py:152
  315.2 6.9 %subtract_divide_fusion = f32[1,6]{0,1:T(8,128)S(1)} fusion(f32[1,6]{0,1:T(8,128)S(1)} %get-tuple-element.254, f32[1,6]{0,1:T(8,128)S(1)} %get-tuple-element.253, f32[1,6]{0,1:T(8,128)S(1)} %get-tuple-element.252, f32[1,6]{0,1:T(8,128)S(1)} %get-tuple-element.251, f32[]{:T(128)} %bitcast.25, f32[]{:T(128)} %bitcast.24, f32[]{:T(128)} %bitcast.20, ...), kind=kLoop, calls=%fused_computation.208 | loop fusion | flops 144 | bytes 212 | tf_op jit(solution)/shard_map/div | solution.py:152
  324.1 4.8 %collective-permute-done.8 = f32[6,3,1,8,128]{4,0,3,2,1:T(8,128)S(1)} collective-permute-done((f32[6,3,1,8,128]{4,0,3,2,1:T(8,128)S(1)}, f32[6,3,1,8,128]{4,0,3,2,1:T(8,128)S(1)}, u32[]{:S(2)}, u32[]{:S(2)}) %collective-permute-start.8) | collective-permute-done | bytes 73760 | tf_op jit(solution)/shard_map/ppermute | solution.py:18
  329.0 2.9 collective-permute-start.9
  331.9 2.7 collective-permute-done.9
  334.6 8.6 %while.39 = (s32[]{:T(128)}, f32[6,4,8,128]{3,2,1,0:T(8,128)S(1)}, f32[6,3,5,9,129]{4,0,3,2,1:T(8,128)S(1)}, s32[]{:T(128)}, f32[24,24,1,1]{1,0,3,2:T(8,128)S(1)}) while((s32[]{:T(128)}, f32[6,4,8,128]{3,2,1,0:T(8,128)S(1)}, f32[6,3,5,9,129]{4,0,3,2,1:T(8,128)S(1)}, s32[]{:T(128)}, f32[24,24,1,1]{1,0,3,2:T(8,128)S(1)}) %tuple.144), condition=%wide.region_10.11_spmd.clone, body=%wide.region_8.10_spmd.sunk.clone.sunk | while | flops 28504064 | bytes 1509813 | solution.py:209
  343.3 2.5 collective-permute-start.10
  347.1 3.2 collective-permute-done.11
  350.3 3.4 collective-permute-start.12
  356.5 2.3 collective-permute-done.13
  359.5 100.5 %psum.7 = f32[]{:T(128)} all-reduce(f32[]{:T(128)} %get-tuple-element.248), channel_id=1, replica_groups=mesh['gx'=32,'gy'=16] {'gx','gy'}, use_global_device_ids=true, to_apply=%region_13.14 | all-reduce | flops 1 | bytes 8 | tf_op jit(solution)/shard_map/psum | solution.py:215
  (323 shorter events, 64.6 us)
Async XLA Ops:
  1.5 6.6 %collective-permute-start = (f32[6,3,1,8,128]{4,3,2,1,0:T(8,128)S(1)}, f32[6,3,1,8,128]{4,3,2,1,0:T(8,128)S(1)}, u32[]{:S(2)}, u32[]{:S(2)}) collective-permute-start(f32[6,3,1,8,128]{4,3,2,1,0:T(8,128)S(1)} %slice.505), channel_id=1, source_target_pairs={{16,0},{32,16},{48,32},{64,48},{80,64},{96,80},{112,96},{128,112},... | collective-permute-start | bytes 221192 | tf_op jit(solution)/shard_map/ppermute | solution.py:18
  8.1 9.3 %collective-permute-start.1 = (f32[6,3,5,1,128]{4,3,2,1,0:T(1,128)S(1)}, f32[6,3,5,1,128]{4,3,2,1,0:T(1,128)S(1)}, u32[]{:S(2)}, u32[]{:S(2)}) collective-permute-start(f32[6,3,5,1,128]{4,3,2,1,0:T(1,128)S(1)} %slice.696), channel_id=1, source_target_pairs={{1,0},{2,1},{3,2},{4,3},{5,4},{6,5},{7,6},{8,7},{9,8},{10,9},{11,1... | collective-permute-start | bytes 138248 | tf_op jit(solution)/shard_map/ppermute | solution.py:18
  17.3 0.7 copy-start.1
  18.0 48.2 %copy-start.4 = (s32[1,1,6,32]{3,1,2,0:T(1,128)S(1)}, s32[1,1,6,32]{3,1,2,0:T(1,128)}, u32[]{:S(2)}) copy-start(s32[1,1,6,32]{3,1,2,0:T(1,128)} %param.15) | copy-start | bytes 2308
  64.3 4.6 copy-start.5
  64.3 3.2 collective-permute-start.2
  66.3 4.7 %copy-start = (f32[6,3,4,8,128]{4,3,2,1,0:T(8,128)S(1)}, f32[6,3,4,8,128]{4,3,2,1,0:T(8,128)}, u32[]{:S(2)}) copy-start(f32[6,3,4,8,128]{4,3,2,1,0:T(8,128)} %param.12) | copy-start | bytes 884740
  67.6 3.4 collective-permute-start.3
  71.6 6.1 %collective-permute-start.4 = (f32[6,3,1,8,128]{4,0,3,2,1:T(8,128)S(1)}, f32[6,3,1,8,128]{4,0,3,2,1:T(8,128)S(1)}, u32[]{:S(2)}, u32[]{:S(2)}) collective-permute-start(f32[6,3,1,8,128]{4,0,3,2,1:T(8,128)S(1)} %fusion.43), channel_id=1, source_target_pairs={{16,0},{32,16},{48,32},{64,48},{80,64},{96,80},{112,96},{128,112},... | collective-permute-start | bytes 221192 | tf_op jit(solution)/shard_map/ppermute | solution.py:18
  77.8 7.3 %collective-permute-start.5 = (f32[6,3,5,1,128]{4,0,3,2,1:T(8,128)S(1)}, f32[6,3,5,1,128]{4,0,3,2,1:T(8,128)S(1)}, u32[]{:S(2)}, u32[]{:S(2)}) collective-permute-start(f32[6,3,5,1,128]{4,0,3,2,1:T(8,128)S(1)} %pad_maximum_fusion.4), channel_id=1, source_target_pairs={{1,0},{2,1},{3,2},{4,3},{5,4},{6,5},{7,6},{8,7},{9,8},{10,9},{11,1... | collective-permute-start | bytes 138248 | tf_op jit(solution)/shard_map/ppermute | solution.py:18
  132.4 2.6 copy-start.2
  133.1 85.7 %collective-permute-start.6 = (f32[6,3,5,1,128]{4,0,3,2,1:T(8,128)}, f32[6,3,5,1,128]{4,0,3,2,1:T(8,128)S(1)}, u32[]{:S(2)}, u32[]{:S(2)}) collective-permute-start(f32[6,3,5,1,128]{4,0,3,2,1:T(8,128)} %slice.519), channel_id=1, source_target_pairs={{0,1},{1,2},{2,3},{3,4},{4,5},{5,6},{6,7},{7,8},{8,9},{9,10},{10,1... | collective-permute-start | bytes 138248 | tf_op jit(solution)/shard_map/ppermute | solution.py:18
  219.7 3.6 collective-permute-start.7
  322.8 6.1 %collective-permute-start.8 = (f32[6,3,1,8,128]{4,0,3,2,1:T(8,128)S(1)}, f32[6,3,1,8,128]{4,0,3,2,1:T(8,128)S(1)}, u32[]{:S(2)}, u32[]{:S(2)}) collective-permute-start(f32[6,3,1,8,128]{4,0,3,2,1:T(8,128)S(1)} %slice.701), channel_id=1, source_target_pairs={{16,0},{32,16},{48,32},{64,48},{80,64},{96,80},{112,96},{128,112},... | collective-permute-start | bytes 221192 | tf_op jit(solution)/shard_map/ppermute | solution.py:18
  329.0 5.5 %collective-permute-start.9 = (f32[6,3,5,1,128]{4,0,3,2,1:T(8,128)S(1)}, f32[6,3,5,1,128]{4,0,3,2,1:T(8,128)S(1)}, u32[]{:S(2)}, u32[]{:S(2)}) collective-permute-start(f32[6,3,5,1,128]{4,0,3,2,1:T(8,128)S(1)} %pad_maximum_fusion.3), channel_id=1, source_target_pairs={{1,0},{2,1},{3,2},{4,3},{5,4},{6,5},{7,6},{8,7},{9,8},{10,9},{11,1... | collective-permute-start | bytes 138248 | tf_op jit(solution)/shard_map/ppermute | solution.py:18
  334.6 126.0 %copy-start.3 = (f32[4,8,128]{2,1,0:T(8,128)S(1)}, f32[4,8,128]{2,1,0:T(8,128)}, u32[]{:S(2)}) copy-start(f32[4,8,128]{2,1,0:T(8,128)} %param.14) | copy-start | bytes 49156
  343.3 3.8 collective-permute-start.10
  345.8 4.5 collective-permute-start.11
  350.3 6.1 %collective-permute-start.12 = (f32[4,4,128]{2,1,0:T(4,128)S(1)}, f32[4,4,128]{2,1,0:T(4,128)S(1)}, u32[]{:S(2)}, u32[]{:S(2)}) collective-permute-start(f32[4,4,128]{2,1,0:T(4,128)S(1)} %get-tuple-element.271), channel_id=1, source_target_pairs={{0,1},{1,2},{2,3},{3,4},{4,5},{5,6},{6,7},{7,8},{8,9},{9,10},{10,1... | collective-permute-start | bytes 24584 | tf_op jit(solution)/shard_map/ppermute | solution.py:29
  353.8 5.0 %collective-permute-start.13 = (f32[4,4,128]{2,1,0:T(4,128)S(1)}, f32[4,4,128]{2,1,0:T(4,128)S(1)}, u32[]{:S(2)}, u32[]{:S(2)}) collective-permute-start(f32[4,4,128]{2,1,0:T(4,128)S(1)} %get-tuple-element.272), channel_id=1, source_target_pairs={{1,0},{2,1},{3,2},{4,3},{5,4},{6,5},{7,6},{8,7},{9,8},{10,9},{11,1... | collective-permute-start | bytes 24584 | tf_op jit(solution)/shard_map/ppermute | solution.py:31
